TPU v7x, 512 devices: a whole 4x4x16 slice. The times are simulated.
512 devices in a mesh: seq: 128 (over x, z, core), head: 4 (over y).
Axes of the slice: x: 4, y: 4, z: 16, core: 2. Of those that a mesh axis runs over, the one named last changes fastest.
Arguments:
- hidden: bfloat16 [32768, 2560], P(('seq', 'head')), may hold values from -6 to 6
- w_values: bfloat16 [2560, 2560], P('seq', 'head'), may hold values from -0.125 to 0.125
- w_gates: bfloat16 [2560, 2560], P('seq', 'head'), may hold values from -0.125 to 0.125
- w_steps: bfloat16 [2560, 40], P('seq', 'head'), may hold values from -0.0625 to 0.0625
- w_states: bfloat16 [2560, 256], P('seq'), may hold values from -0.125 to 0.125
- conv_weight: float32 [4, 2816], replicated, may hold values from -3 to 3
- conv_bias: float32 [2816], replicated, may hold values from -3 to 3
- step_bias: float32 [40], P('head'), may hold values from -1 to 0.5
- decay_rate: float32 [40], P('head'), may hold values from 0 to 1, as said below
- skip_gain: float32 [40], P('head'), may hold values from 1 to 8
- norm_gain: float32 [2560], replicated, may hold values from 0.5 to 1.5
- lengths: int32 [64], replicated, may hold values from 256 to 768, as said below
Outputs:
- gated_out: bfloat16 [32768, 2560], P(('seq', 'head'))
- final_states: float32 [128, 40, 64, 128], P('seq', 'head')
Inputs may be any that keep to these rules, and one draw needn't show every extreme that they name: Prompts are packed in order, each holding 256 to 768 tokens; the lengths sum to 32768. `decay_rate`: positive rates.
All inputs are finite; a program needn't handle non-finite values.
Results may differ from a plain program's by a relative error of at most 0.01.
Values may be sent and summed in bfloat16 or wider, within the bound.
No kernel may reach another device: no remote copies, remote signals or barrier semaphores. Data moves between devices by JAX's collectives and lax.ppermute only.
A program may use at most 128 MiB of HBM per device.

v0:
```python
import jax
import jax.numpy as jnp
from jax import lax
from jax.sharding import PartitionSpec as P

STRETCH = 256
epsilon = 1e-05


def from_behind(block, axis, distance):
    devices = range(lax.axis_size(axis))
    route = [(i - distance, i) for i in devices if i - distance in devices]
    return lax.ppermute(block, axis, route)


def segments_at(positions, prompt_ends):
    counted = jnp.sum((prompt_ends[None, :] <= positions[:, None]).astype(jnp.int32), axis=1)
    return jnp.where(positions < 0, -1, counted)


def on_device(
    hidden,
    w_values,
    w_gates,
    w_steps,
    w_states,
    conv_weight,
    conv_bias,
    step_bias,
    decay_rate,
    skip_gain,
    norm_gain,
    lengths,
):
    groups = lax.axis_size("head")
    group_index = lax.axis_index("head")
    block_index = lax.axis_index("seq")
    local_width = w_values.shape[1]
    inner_width = local_width * groups
    local_heads = decay_rate.shape[0]
    head_width = local_width // local_heads
    state_width = w_states.shape[1] // 2
    conv_taps = conv_weight.shape[0]
    prompt_ends = jnp.cumsum(lengths)
    block_hidden = lax.all_to_all(
        jnp.broadcast_to(hidden[None], (groups,) + hidden.shape), "head", 0, 0, tiled=True
    ).reshape(groups * hidden.shape[0], hidden.shape[1])
    block_rows = block_hidden.shape[0]
    sub_rows = block_rows // groups
    step_width = w_steps.shape[1]
    merged = jnp.concatenate([w_values, w_states, w_gates, w_steps], axis=1)
    full = lax.all_gather(merged, "seq", axis=0, tiled=True)
    projected = jnp.dot(block_hidden, full, preferred_element_type=jnp.float32)
    conv_end = local_width + 2 * state_width
    pre_rows = projected[:, :conv_end].astype(jnp.bfloat16)
    gates_sum = projected[:, conv_end : conv_end + local_width]
    steps_sum = projected[:, conv_end + local_width : conv_end + local_width + step_width]
    local_taps = jnp.concatenate(
        [
            lax.dynamic_slice_in_dim(conv_weight, group_index * local_width, local_width, 1),
            conv_weight[:, inner_width:],
        ],
        axis=1,
    )
    local_bias = jnp.concatenate(
        [
            lax.dynamic_slice_in_dim(conv_bias, group_index * local_width, local_width, 0),
            conv_bias[inner_width:],
        ],
        axis=0,
    )
    block_start = block_index * block_rows
    rim_rows = pre_rows[block_rows - (conv_taps - 1) :]
    prior_rim = from_behind(rim_rows, "seq", 1)
    extended = jnp.concatenate([prior_rim, pre_rows], axis=0)
    ext_positions = (
        block_start - (conv_taps - 1) + jnp.arange(block_rows + conv_taps - 1, dtype=jnp.int32)
    )
    ext_ids = segments_at(ext_positions, prompt_ends)
    own_ids = ext_ids[conv_taps - 1 :]
    filtered = jnp.zeros(pre_rows.shape, jnp.float32) + local_bias[None, :]
    for offset in range(conv_taps):
        matches = (ext_ids[offset : offset + block_rows] == own_ids).astype(jnp.float32)
        filtered = (
            filtered
            + local_taps[offset][None, :]
            * extended[offset : offset + block_rows].astype(jnp.float32)
            * matches[:, None]
        )
    conv_out = jax.nn.silu(filtered).astype(jnp.bfloat16)
    head_values = conv_out[:, :local_width]
    both_states = conv_out[:, local_width:]
    stretch_rows = STRETCH
    stretches = block_rows // stretch_rows
    positions = block_start + jnp.arange(block_rows, dtype=jnp.int32)
    segment_ids = segments_at(positions, prompt_ends)
    next_ids = segments_at(positions + 1, prompt_ends)
    before_ids = segments_at(positions - 1, prompt_ends)
    stretch_ids = segment_ids.reshape(stretches, stretch_rows)
    prior_ids = before_ids.reshape(stretches, stretch_rows)[:, 0]
    ends_mask = (segment_ids != next_ids).reshape(stretches, stretch_rows)
    step_sizes = jax.nn.softplus(steps_sum + step_bias[None, :])
    decay_steps = step_sizes * decay_rate[None, :]
    log_decay = -jnp.cumsum(decay_steps.reshape(stretches, stretch_rows, local_heads), axis=1)
    decay_heads = jnp.swapaxes(log_decay, 1, 2)
    step_heads = jnp.swapaxes(step_sizes.reshape(stretches, stretch_rows, local_heads), 1, 2)
    values = head_values.reshape(stretches, stretch_rows, local_heads, head_width)
    write_state = both_states[:, :state_width].reshape(stretches, stretch_rows, state_width)
    read_state = both_states[:, state_width:].reshape(stretches, stretch_rows, state_width)
    intersection = jnp.einsum(
        "ctn,csn->cts", read_state, write_state, preferred_element_type=jnp.float32
    )
    token_order = jnp.arange(stretch_rows, dtype=jnp.int32)
    causal = token_order[:, None] >= token_order[None, :]
    allowed = causal[None] & (stretch_ids[:, :, None] == stretch_ids[:, None, :])
    spread = decay_heads[:, :, :, None] - decay_heads[:, :, None, :]
    weights = (
        jnp.where(allowed[:, None], jnp.exp(jnp.minimum(spread, 0.0)), 0.0)
        * step_heads[:, :, None, :]
    )
    scores = (intersection[:, None] * weights).astype(jnp.bfloat16)
    within_stretch = jnp.einsum(
        "chts,cshp->cthp", scores, values, preferred_element_type=jnp.float32
    )
    last_ids = stretch_ids[:, -1]
    tail_decay = decay_heads[:, :, -1:]
    keep_tail = (stretch_ids == last_ids[:, None])[:, None, :]
    tail_coef = (
        jnp.where(keep_tail, jnp.exp(jnp.minimum(tail_decay - decay_heads, 0.0)), 0.0) * step_heads
    )
    tail_rows = (values.astype(jnp.float32) * jnp.swapaxes(tail_coef, 1, 2)[:, :, :, None]).astype(
        jnp.bfloat16
    )
    stretch_states = jnp.einsum(
        "clhp,cln->chpn", tail_rows, write_state, preferred_element_type=jnp.float32
    )
    stretch_gates = (
        jnp.exp(decay_heads[:, :, -1]) * (last_ids == prior_ids).astype(jnp.float32)[:, None]
    )
    own_pair = (stretch_gates[0], stretch_states[0])
    g1, s1 = from_behind(own_pair, "seq", 1)
    g2, s2 = from_behind(own_pair, "seq", 2)
    g3, s3 = from_behind(own_pair, "seq", 3)
    incoming = s1 + g1[:, None, None] * (s2 + g2[:, None, None] * s3)
    arriving = incoming[None]
    carry_mask = (stretch_ids == prior_ids[:, None]).astype(jnp.float32)
    carry_decay = jnp.exp(log_decay) * carry_mask[:, :, None]
    from_before = (
        jnp.einsum(
            "cln,chpn->clhp",
            read_state,
            arriving.astype(jnp.bfloat16),
            preferred_element_type=jnp.float32,
        )
        * carry_decay[:, :, :, None]
    )
    result = (
        within_stretch + from_before + skip_gain[None, None, :, None] * values.astype(jnp.float32)
    )
    ssm_rows = result.reshape(block_rows, local_width).astype(jnp.bfloat16)
    end_weight = ends_mask.astype(jnp.float32)
    has_end = jnp.sum(end_weight, axis=1)
    end_decay = jnp.sum(decay_heads * end_weight[:, None, :], axis=2)
    end_ids = jnp.sum(jnp.where(ends_mask, stretch_ids, 0), axis=1)
    keep_end = ((stretch_ids == end_ids[:, None]) & (has_end[:, None] > 0))[:, None, :]
    end_coef = (
        jnp.where(keep_end, jnp.exp(jnp.minimum(end_decay[:, :, None] - decay_heads, 0.0)), 0.0)
        * step_heads
    )
    end_rows = (values.astype(jnp.float32) * jnp.swapaxes(end_coef, 1, 2)[:, :, :, None]).astype(
        jnp.bfloat16
    )
    end_states = jnp.einsum(
        "clhp,cln->chpn", end_rows, write_state, preferred_element_type=jnp.float32
    )
    end_carry = (
        jnp.exp(end_decay) * ((end_ids == prior_ids) & (has_end > 0)).astype(jnp.float32)[:, None]
    )
    end_states = end_states + end_carry[:, :, None, None] * arriving
    final_block = jnp.sum(end_states, axis=0)[None]
    head_gates = gates_sum.astype(jnp.bfloat16)
    both = jnp.stack([ssm_rows, head_gates]).reshape(2, groups, sub_rows, local_width)
    returned = lax.all_to_all(both, "head", split_axis=1, concat_axis=3, tiled=True)
    token_rows = returned.reshape(2, sub_rows, inner_width).astype(jnp.float32)
    gated = token_rows[0] * jax.nn.silu(token_rows[1])
    mean_square = jnp.mean(gated * gated, axis=1)
    scaled = gated * lax.rsqrt(mean_square + epsilon)[:, None] * norm_gain[None, :]
    gated_out = scaled.astype(jnp.bfloat16)
    return (gated_out, final_block)


def solution(mesh):
    in_specs = (
        P(("seq", "head"), None),
        P("seq", "head"),
        P("seq", "head"),
        P("seq", "head"),
        P("seq", None),
        P(),
        P(),
        P("head"),
        P("head"),
        P("head"),
        P(),
        P(),
    )
    out_specs = (P(("seq", "head"), None), P("seq", "head", None, None))
    return jax.shard_map(
        on_device, mesh=mesh, in_specs=in_specs, out_specs=out_specs, check_vma=False
    )
```

profile of v0, /device:TPU:5, one launch (start us, length us, event | category | flops | bytes accessed | tf_op | source)
XLA Modules:
  0.0 259.8 jit_solution(16076834221550302030)
XLA Ops:
  8.0 1.4 maximum_bitcast_fusion
  9.5 2.1 broadcast_in_dim.39
  11.6 4.3 %all-to-all-start = ((bf16[4,64,2560]{2,1,0:T(8,128)(2,1)}), bf16[4,64,2560]{2,1,0:T(8,128)(2,1)S(1)}, u32[]{:S(2)}, u32[]{:S(2)}) async-start(bf16[4,64,2560]{2,1,0:T(8,128)(2,1)} %broadcast_in_dim.39), calls=%async_computation | async-start | bytes 2621440 | tf_op jit(solution)/shard_map/all_to_all | solution.py:45
  25.1 139.3 %all-gather.3.cloned.1.call-done = bf16[128,20,1546]{2,1,0:T(8,128)(2,1)} async-done(((bf16[1,20,1546]{2,1,0:T(8,128)(2,1)}), bf16[128,20,1546]{2,1,0:T(8,128)(2,1)}) %all-gather.3.cloned.1.call-update) | async-done | bytes 7915536 | tf_op jit(solution)/shard_map/all_gather | solution.py:52
  164.5 13.7 %reshape.504 = bf16[2560,1546]{1,0:T(8,128)(2,1)} reshape(bf16[128,20,1546]{2,1,0:T(8,128)(2,1)} %all-gather.3.cloned.1.call-done) | data formatting | bytes 15831040
  178.2 5.8 %fusion.50 = (bf16[256,1546]{0,1:T(8,128)(2,1)S(1)}, f32[256,1546]{0,1:T(8,128)S(1)}) fusion(bf16[2560,1546]{1,0:T(8,128)(2,1)} %reshape.504, bf16[256,2560]{1,0:T(8,128)(2,1)S(1)} %bitcast.126), kind=kOutput, calls=%fused_computation.113 | convolution fusion | flops 2026768896 | bytes 11600896 | tf_op jit(solution)/shard_map/dot_general | solution.py:53
  184.2 1.0 copy-done.4
  187.4 3.4 %collective-permute-start.4 = (f32[10]{0:T(128)S(1)}, f32[10]{0:T(128)S(1)}, u32[]{:S(2)}, u32[]{:S(2)}) collective-permute-start(f32[10]{0:T(128)S(1)} %exponential_multiply_fusion.1), channel_id=1, source_target_pairs={{0,8},{4,12},{8,16},{12,20},{16,24},{20,28},{24,32},{28,36},{32,40... | collective-permute-start | bytes 128 | tf_op jit(solution)/shard_map/ppermute | solution.py:13
  190.8 2.8 %collective-permute-start.2 = (f32[10]{0:T(128)S(1)}, f32[10]{0:T(128)S(1)}, u32[]{:S(2)}, u32[]{:S(2)}) collective-permute-start(f32[10]{0:T(128)S(1)} %exponential_multiply_fusion.1), channel_id=1, source_target_pairs={{0,4},{4,8},{8,12},{12,16},{16,20},{20,24},{24,28},{28,32},{32,36}... | collective-permute-start | bytes 128 | tf_op jit(solution)/shard_map/ppermute | solution.py:13
  193.8 1.9 collective-permute-start
  197.7 0.9 collective-permute-done
  198.7 1.5 multiply_convert_fusion.4
  201.3 4.4 %collective-permute-start.1 = (f32[10,64,128]{2,1,0:T(8,128)S(1)}, f32[10,64,128]{2,1,0:T(8,128)S(1)}, u32[]{:S(2)}, u32[]{:S(2)}) collective-permute-start(f32[10,64,128]{2,1,0:T(8,128)S(1)} %fusion.20), channel_id=1, source_target_pairs={{0,4},{4,8},{8,12},{12,16},{16,20},{20,24},{24,28},{28,32},{32,36}... | collective-permute-start | bytes 983048 | tf_op jit(solution)/shard_map/ppermute | solution.py:13
  205.7 3.0 %collective-permute-start.3 = (f32[10,64,128]{2,1,0:T(8,128)S(1)}, f32[10,64,128]{2,1,0:T(8,128)S(1)}, u32[]{:S(2)}, u32[]{:S(2)}) collective-permute-start(f32[10,64,128]{2,1,0:T(8,128)S(1)} %fusion.20), channel_id=1, source_target_pairs={{0,8},{4,12},{8,16},{12,20},{16,24},{20,28},{24,32},{28,36},{32,40... | collective-permute-start | bytes 983048 | tf_op jit(solution)/shard_map/ppermute | solution.py:13
  208.7 2.5 collective-permute-start.5
  211.4 0.9 fusion.7
  212.4 11.8 %collective-permute-done.3 = f32[10,64,128]{2,1,0:T(8,128)S(1)} collective-permute-done((f32[10,64,128]{2,1,0:T(8,128)S(1)}, f32[10,64,128]{2,1,0:T(8,128)S(1)}, u32[]{:S(2)}, u32[]{:S(2)}) %collective-permute-start.3) | collective-permute-done | bytes 327712 | tf_op jit(solution)/shard_map/ppermute | solution.py:13
  224.2 7.7 %collective-permute-done.5 = f32[10,64,128]{2,1,0:T(8,128)S(1)} collective-permute-done((f32[10,64,128]{2,1,0:T(8,128)S(1)}, f32[10,64,128]{2,1,0:T(8,128)S(1)}, u32[]{:S(2)}, u32[]{:S(2)}) %collective-permute-start.5) | collective-permute-done | bytes 327712 | tf_op jit(solution)/shard_map/ppermute | solution.py:13
  232.6 1.1 pad_maximum_fusion
  233.7 2.4 copy.76
  236.1 4.0 %all-to-all-start.1 = ((bf16[2,4,64,640]{3,2,0,1:T(8,128)(2,1)}), bf16[2,4,64,640]{3,2,0,1:T(8,128)(2,1)S(1)}, u32[]{:S(2)}, u32[]{:S(2)}) async-start(bf16[2,4,64,640]{3,2,0,1:T(8,128)(2,1)} %copy.76), calls=%async_computation.1 | async-start | bytes 1310720 | tf_op jit(solution)/shard_map/all_to_all | solution.py:183
  240.8 1.0 add_bitcast_fusion
  241.8 8.4 %all-to-all-done.1 = bf16[2,4,64,640]{3,2,0,1:T(8,128)(2,1)S(1)} async-done(((bf16[2,4,64,640]{3,2,0,1:T(8,128)(2,1)}), bf16[2,4,64,640]{3,2,0,1:T(8,128)(2,1)S(1)}, u32[]{:S(2)}, u32[]{:S(2)}) %all-to-all-start.1) | async-done | bytes 655392 | tf_op jit(solution)/shard_map/all_to_all | solution.py:183
  252.1 0.8 multiply_convert_fusion.5
  (92 shorter events, 14.9 us)
Async XLA Ops:
  7.2 157.3 %all-gather.3.cloned.1.call-start = ((), (), s32[]{:S(2)}) async-start(), calls=%async_computation.2 | async-start | bytes 10303488 | tf_op jit(solution)/shard_map/all_gather | solution.py:52
  11.6 4.3 %copy-start.5 = (s32[64]{0:T(128)S(1)}, s32[64]{0:T(128)}, u32[]{:S(2)}) copy-start(s32[64]{0:T(128)} %param.23) | copy-start | bytes 772
  11.6 11.8 %copy-start.1 = (f32[4,2816]{1,0:T(4,128)S(1)}, f32[4,2816]{1,0:T(4,128)}, u32[]{:S(2)}) copy-start(f32[4,2816]{1,0:T(4,128)} %param.17) | copy-start | bytes 135172
  11.6 11.8 %slice-start = ((f32[4,2816]{1,0:T(4,128)}), f32[4,256]{1,0:T(4,128)S(1)}, s32[]{:S(2)}) async-start(f32[4,2816]{1,0:T(4,128)} %param.17), calls=%async_computation.3 | async-start | bytes 8192 | tf_op jit(solution)/shard_map/slice | solution.py:61
  11.6 166.6 %all-to-all-start = ((bf16[4,64,2560]{2,1,0:T(8,128)(2,1)}), bf16[4,64,2560]{2,1,0:T(8,128)(2,1)S(1)}, u32[]{:S(2)}, u32[]{:S(2)}) async-start(bf16[4,64,2560]{2,1,0:T(8,128)(2,1)} %broadcast_in_dim.39), calls=%async_computation | async-start | bytes 2621440 | tf_op jit(solution)/shard_map/all_to_all | solution.py:45
  178.2 5.9 %copy-start.3 = (f32[10]{0:T(128)S(1)}, f32[10]{0:T(128)}, u32[]{:S(2)}) copy-start(f32[10]{0:T(128)} %param.19) | copy-start | bytes 124
  178.2 5.9 %copy-start.6 = (f32[10]{0:T(128)S(1)}, f32[10]{0:T(128)}, u32[]{:S(2)}) copy-start(f32[10]{0:T(128)} %param.20) | copy-start | bytes 124
  184.0 1.2 copy-start.4
  187.4 24.9 %collective-permute-start.4 = (f32[10]{0:T(128)S(1)}, f32[10]{0:T(128)S(1)}, u32[]{:S(2)}, u32[]{:S(2)}) collective-permute-start(f32[10]{0:T(128)S(1)} %exponential_multiply_fusion.1), channel_id=1, source_target_pairs={{0,8},{4,12},{8,16},{12,20},{16,24},{20,28},{24,32},{28,36},{32,40... | collective-permute-start | bytes 128 | tf_op jit(solution)/shard_map/ppermute | solution.py:13
  190.8 21.5 %collective-permute-start.2 = (f32[10]{0:T(128)S(1)}, f32[10]{0:T(128)S(1)}, u32[]{:S(2)}, u32[]{:S(2)}) collective-permute-start(f32[10]{0:T(128)S(1)} %exponential_multiply_fusion.1), channel_id=1, source_target_pairs={{0,4},{4,8},{8,12},{12,16},{16,20},{20,24},{24,28},{28,32},{32,36}... | collective-permute-start | bytes 128 | tf_op jit(solution)/shard_map/ppermute | solution.py:13
  193.8 4.9 %collective-permute-start = (bf16[3,896]{0,1:T(8,128)(2,1)S(1)}, bf16[3,896]{0,1:T(8,128)(2,1)S(1)}, u32[]{:S(2)}, u32[]{:S(2)}) collective-permute-start(bf16[3,896]{0,1:T(8,128)(2,1)S(1)} %slice.120), channel_id=1, source_target_pairs={{0,4},{4,8},{8,12},{12,16},{16,20},{20,24},{24,28},{28,32},{32,36}... | collective-permute-start | bytes 16136 | tf_op jit(solution)/shard_map/ppermute | solution.py:13
  201.3 11.0 %collective-permute-start.1 = (f32[10,64,128]{2,1,0:T(8,128)S(1)}, f32[10,64,128]{2,1,0:T(8,128)S(1)}, u32[]{:S(2)}, u32[]{:S(2)}) collective-permute-start(f32[10,64,128]{2,1,0:T(8,128)S(1)} %fusion.20), channel_id=1, source_target_pairs={{0,4},{4,8},{8,12},{12,16},{16,20},{20,24},{24,28},{28,32},{32,36}... | collective-permute-start | bytes 983048 | tf_op jit(solution)/shard_map/ppermute | solution.py:13
  205.7 18.5 %collective-permute-start.3 = (f32[10,64,128]{2,1,0:T(8,128)S(1)}, f32[10,64,128]{2,1,0:T(8,128)S(1)}, u32[]{:S(2)}, u32[]{:S(2)}) collective-permute-start(f32[10,64,128]{2,1,0:T(8,128)S(1)} %fusion.20), channel_id=1, source_target_pairs={{0,8},{4,12},{8,16},{12,20},{16,24},{20,28},{24,32},{28,36},{32,40... | collective-permute-start | bytes 983048 | tf_op jit(solution)/shard_map/ppermute | solution.py:13
  208.7 23.2 %collective-permute-start.5 = (f32[10,64,128]{2,1,0:T(8,128)S(1)}, f32[10,64,128]{2,1,0:T(8,128)S(1)}, u32[]{:S(2)}, u32[]{:S(2)}) collective-permute-start(f32[10,64,128]{2,1,0:T(8,128)S(1)} %fusion.20), channel_id=1, source_target_pairs={{0,12},{4,16},{8,20},{12,24},{16,28},{20,32},{24,36},{28,40},{32,4... | collective-permute-start | bytes 983048 | tf_op jit(solution)/shard_map/ppermute | solution.py:13
  211.4 20.7 %copy-start.7 = (f32[10]{0:T(128)S(1)}, f32[10]{0:T(128)}, u32[]{:S(2)}) copy-start(f32[10]{0:T(128)} %param.21) | copy-start | bytes 124
  233.7 7.1 %copy-start = (bf16[256,640]{0,1:T(8,128)(2,1)S(1)}, bf16[256,640]{0,1:T(8,128)(2,1)}, u32[]{:S(2)}) copy-start(bf16[256,640]{0,1:T(8,128)(2,1)} %get-tuple-element.20) | copy-start | bytes 983044
  236.1 14.1 %all-to-all-start.1 = ((bf16[2,4,64,640]{3,2,0,1:T(8,128)(2,1)}), bf16[2,4,64,640]{3,2,0,1:T(8,128)(2,1)S(1)}, u32[]{:S(2)}, u32[]{:S(2)}) async-start(bf16[2,4,64,640]{3,2,0,1:T(8,128)(2,1)} %copy.76), calls=%async_computation.1 | async-start | bytes 1310720 | tf_op jit(solution)/shard_map/all_to_all | solution.py:183
  251.4 0.7 copy-start.2
Sparse Core Ops, SparseCore 0:
  11.7 152.7 all-gather.2
where the time goes:
time: 261 us; the launch traced here: 260 us
  waiting for transfers between devices  168 us (64%)
  local copies, waits for them, and re-layouts  26.9 us (10%)
  starting transfers between devices  26.3 us (10%)
  between operations  18.4 us (7%)
  other arithmetic  11.4 us (4%)
  matrix products  8.44 us (3%)
    all_gather x1, waiting for transfers between devices, on_device(): full = lax.all_gather(merged, 'seq', axis=0, tiled=True)  139 us
    ppermute x6, waiting for transfers between devices, from_behind(): return lax.ppermute(block, axis, route)  20.5 us
    ppermute x6, starting transfers between devices, from_behind(): return lax.ppermute(block, axis, route)  18 us
    unnamed x24, local copies, waits for them, and re-layouts  16 us
    all_to_all x1, waiting for transfers between devices, on_device(): lax.all_to_all(both, 'head', split_axis=1, concat_axis=3, tiled=True)  8.45 us
    dot_general x1, matrix products, on_device(): projected = jnp.dot(block_hidden, full, preferred_element_type=jnp.float32)  5.84 us
  transfers between devices with their start and end apart: 9, of which 5 were waited for; matrix products, arithmetic and copies ran while one was open for 11% of the time, Pallas kernels for 0%

commit v1 on v0

--- a/solution.py
+++ b/solution.py
@@ -49,7 +49,9 @@
     sub_rows = block_rows // groups
     step_width = w_steps.shape[1]
     merged = jnp.concatenate([w_values, w_states, w_gates, w_steps], axis=1)
-    full = lax.all_gather(merged, "seq", axis=0, tiled=True)
+    full = jnp.concatenate(
+        lax.all_to_all(jnp.stack([merged] * lax.axis_size("seq")), "seq", 0, 0), axis=0
+    )
     projected = jnp.dot(block_hidden, full, preferred_element_type=jnp.float32)
     conv_end = local_width + 2 * state_width
     pre_rows = projected[:, :conv_end].astype(jnp.bfloat16)

time: 261 us -> 569 us (2.18)
  the two profiles are of different devices: /device:TPU:5 before, /device:TPU:3 now
where the time goes in v1:
time: 569 us; the launch traced here: 568 us
  waiting for transfers between devices  460 us (81%)
  starting transfers between devices  53 us (9%)
  local copies, waits for them, and re-layouts  30.5 us (5%)
  other arithmetic  10.8 us (2%)
  matrix products  8.43 us (1%)
    all_to_all x1, waiting for transfers between devices, on_device(): lax.all_to_all(jnp.stack([merged] * lax.axis_size('seq')), 'seq', 0, 0)  433 us
    ppermute x6, starting transfers between devices, from_behind(): return lax.ppermute(block, axis, route)  25 us
    all_to_all x1, starting transfers between devices, on_device(): lax.all_to_all(jnp.stack([merged] * lax.axis_size('seq')), 'seq', 0, 0)  20.4 us
    ppermute x6, waiting for transfers between devices, from_behind(): return lax.ppermute(block, axis, route)  19.1 us
    reshape x1, local copies, waits for them, and re-layouts, on_device(): jnp.concatenate(lax.all_to_all(jnp.stack([merged] * lax.axis_size('seq'))...  13.7 us
  transfers between devices with their start and end apart: 9, of which 5 were waited for; matrix products, arithmetic and copies ran while one was open for 5% of the time, Pallas kernels for 0%

profile of v1, /device:TPU:3, one launch (start us, length us, event | category | flops | bytes accessed | tf_op | source)
XLA Modules:
  0.0 568.1 jit_solution(8997134225011356284)
XLA Ops:
  2.2 4.5 stack.6
  6.8 20.4 %all-to-all-start = ((bf16[128,20,1546]{2,1,0:T(8,128)(2,1)}), bf16[128,20,1546]{2,1,0:T(8,128)(2,1)}, u32[]{:S(2)}, u32[]{:S(2)}) async-start(bf16[128,20,1546]{2,1,0:T(8,128)(2,1)} %stack.6), calls=%async_computation | async-start | bytes 20447232 | tf_op jit(solution)/shard_map/all_to_all | solution.py:53
  35.6 433.5 %all-to-all-done = bf16[128,20,1546]{2,1,0:T(8,128)(2,1)} async-done(((bf16[128,20,1546]{2,1,0:T(8,128)(2,1)}), bf16[128,20,1546]{2,1,0:T(8,128)(2,1)}, u32[]{:S(2)}, u32[]{:S(2)}) %all-to-all-start) | async-done | bytes 7915552 | tf_op jit(solution)/shard_map/all_to_all | solution.py:53
  469.1 1.2 broadcast_in_dim.39
  470.2 4.2 all-to-all-start.1
  475.3 13.7 %reshape.491 = bf16[2560,1546]{1,0:T(8,128)(2,1)} reshape(bf16[128,20,1546]{2,1,0:T(8,128)(2,1)} %all-to-all-done) | data formatting | bytes 15831040 | tf_op jit(solution)/shard_map/reshape | solution.py:52
  489.0 5.8 %fusion.50 = (bf16[256,1546]{0,1:T(8,128)(2,1)S(1)}, f32[256,1546]{0,1:T(8,128)S(1)}) fusion(bf16[2560,1546]{1,0:T(8,128)(2,1)} %reshape.491, bf16[256,2560]{1,0:T(8,128)(2,1)S(1)} %bitcast.124), kind=kOutput, calls=%fused_computation.113 | convolution fusion | flops 2026768896 | bytes 11600896 | tf_op jit(solution)/shard_map/dot_general | solution.py:55
  495.0 1.0 copy-done.5
  498.2 6.7 %collective-permute-start.4 = (f32[10]{0:T(128)S(1)}, f32[10]{0:T(128)S(1)}, u32[]{:S(2)}, u32[]{:S(2)}) collective-permute-start(f32[10]{0:T(128)S(1)} %exponential_multiply_fusion.1), channel_id=1, source_target_pairs={{0,8},{4,12},{8,16},{12,20},{16,24},{20,28},{24,32},{28,36},{32,40... | collective-permute-start | bytes 128 | tf_op jit(solution)/shard_map/ppermute | solution.py:13
  504.9 4.3 collective-permute-start.2
  509.4 1.9 collective-permute-start
  513.3 0.9 collective-permute-done
  514.3 1.5 multiply_convert_fusion.4
  516.9 4.9 collective-permute-start.1
  521.9 4.9 collective-permute-start.3
  526.8 2.2 collective-permute-start.5
  529.2 0.9 fusion.7
  530.2 11.2 %collective-permute-done.3 = f32[10,64,128]{2,1,0:T(8,128)S(1)} collective-permute-done((f32[10,64,128]{2,1,0:T(8,128)S(1)}, f32[10,64,128]{2,1,0:T(8,128)S(1)}, u32[]{:S(2)}, u32[]{:S(2)}) %collective-permute-start.3) | collective-permute-done | bytes 327712 | tf_op jit(solution)/shard_map/ppermute | solution.py:13
  541.4 7.0 %collective-permute-done.5 = f32[10,64,128]{2,1,0:T(8,128)S(1)} collective-permute-done((f32[10,64,128]{2,1,0:T(8,128)S(1)}, f32[10,64,128]{2,1,0:T(8,128)S(1)}, u32[]{:S(2)}, u32[]{:S(2)}) %collective-permute-start.5) | collective-permute-done | bytes 327712 | tf_op jit(solution)/shard_map/ppermute | solution.py:13
  549.0 1.1 pad_maximum_fusion
  550.1 2.4 copy.76
  552.5 3.5 all-to-all-start.2
  556.6 1.0 add_bitcast_fusion
  557.6 7.8 %all-to-all-done.2 = bf16[2,4,64,640]{3,2,0,1:T(8,128)(2,1)S(1)} async-done(((bf16[2,4,64,640]{3,2,0,1:T(8,128)(2,1)}), bf16[2,4,64,640]{3,2,0,1:T(8,128)(2,1)S(1)}, u32[]{:S(2)}, u32[]{:S(2)}) %all-to-all-start.2) | async-done | bytes 655392 | tf_op jit(solution)/shard_map/all_to_all | solution.py:185
  (94 shorter events, 16.5 us)
Async XLA Ops:
  6.7 20.4 %copy-start.6 = (s32[64]{0:T(128)S(1)}, s32[64]{0:T(128)}, u32[]{:S(2)}) copy-start(s32[64]{0:T(128)} %param.23) | copy-start | bytes 772
  6.7 28.0 %copy-start.2 = (f32[4,2816]{1,0:T(4,128)S(1)}, f32[4,2816]{1,0:T(4,128)}, u32[]{:S(2)}) copy-start(f32[4,2816]{1,0:T(4,128)} %param.17) | copy-start | bytes 135172
  6.7 28.0 %slice-start = ((f32[4,2816]{1,0:T(4,128)}), f32[4,256]{1,0:T(4,128)S(1)}, s32[]{:S(2)}) async-start(f32[4,2816]{1,0:T(4,128)} %param.17), calls=%async_computation.3 | async-start | bytes 8192 | tf_op jit(solution)/shard_map/slice | solution.py:63
  6.7 462.3 %copy-start.1 = (bf16[64,2560]{1,0:T(8,128)(2,1)S(1)}, bf16[64,2560]{1,0:T(8,128)(2,1)}, u32[]{:S(2)}) copy-start(bf16[64,2560]{1,0:T(8,128)(2,1)} %param.12) | copy-start | bytes 983044
  6.8 462.3 %all-to-all-start = ((bf16[128,20,1546]{2,1,0:T(8,128)(2,1)}), bf16[128,20,1546]{2,1,0:T(8,128)(2,1)}, u32[]{:S(2)}, u32[]{:S(2)}) async-start(bf16[128,20,1546]{2,1,0:T(8,128)(2,1)} %stack.6), calls=%async_computation | async-start | bytes 20447232 | tf_op jit(solution)/shard_map/all_to_all | solution.py:53
  470.2 18.8 %all-to-all-start.1 = ((bf16[4,64,2560]{2,1,0:T(8,128)(2,1)}), bf16[4,64,2560]{2,1,0:T(8,128)(2,1)S(1)}, u32[]{:S(2)}, u32[]{:S(2)}) async-start(bf16[4,64,2560]{2,1,0:T(8,128)(2,1)} %broadcast_in_dim.39), calls=%async_computation.1 | async-start | bytes 2621440 | tf_op jit(solution)/shard_map/all_to_all | solution.py:45
  489.0 5.9 %copy-start.4 = (f32[10]{0:T(128)S(1)}, f32[10]{0:T(128)}, u32[]{:S(2)}) copy-start(f32[10]{0:T(128)} %param.19) | copy-start | bytes 124
  489.0 5.9 %copy-start.7 = (f32[10]{0:T(128)S(1)}, f32[10]{0:T(128)}, u32[]{:S(2)}) copy-start(f32[10]{0:T(128)} %param.20) | copy-start | bytes 124
  494.8 1.2 copy-start.5
  498.2 31.9 %collective-permute-start.4 = (f32[10]{0:T(128)S(1)}, f32[10]{0:T(128)S(1)}, u32[]{:S(2)}, u32[]{:S(2)}) collective-permute-start(f32[10]{0:T(128)S(1)} %exponential_multiply_fusion.1), channel_id=1, source_target_pairs={{0,8},{4,12},{8,16},{12,20},{16,24},{20,28},{24,32},{28,36},{32,40... | collective-permute-start | bytes 128 | tf_op jit(solution)/shard_map/ppermute | solution.py:13
  504.9 25.2 %collective-permute-start.2 = (f32[10]{0:T(128)S(1)}, f32[10]{0:T(128)S(1)}, u32[]{:S(2)}, u32[]{:S(2)}) collective-permute-start(f32[10]{0:T(128)S(1)} %exponential_multiply_fusion.1), channel_id=1, source_target_pairs={{0,4},{4,8},{8,12},{12,16},{16,20},{20,24},{24,28},{28,32},{32,36}... | collective-permute-start | bytes 128 | tf_op jit(solution)/shard_map/ppermute | solution.py:13
  509.4 4.9 collective-permute-start
  516.9 13.2 %collective-permute-start.1 = (f32[10,64,128]{2,1,0:T(8,128)S(1)}, f32[10,64,128]{2,1,0:T(8,128)S(1)}, u32[]{:S(2)}, u32[]{:S(2)}) collective-permute-start(f32[10,64,128]{2,1,0:T(8,128)S(1)} %fusion.20), channel_id=1, source_target_pairs={{0,4},{4,8},{8,12},{12,16},{16,20},{20,24},{24,28},{28,32},{32,36}... | collective-permute-start | bytes 983048 | tf_op jit(solution)/shard_map/ppermute | solution.py:13
  521.9 19.5 %collective-permute-start.3 = (f32[10,64,128]{2,1,0:T(8,128)S(1)}, f32[10,64,128]{2,1,0:T(8,128)S(1)}, u32[]{:S(2)}, u32[]{:S(2)}) collective-permute-start(f32[10,64,128]{2,1,0:T(8,128)S(1)} %fusion.20), channel_id=1, source_target_pairs={{0,8},{4,12},{8,16},{12,20},{16,24},{20,28},{24,32},{28,36},{32,40... | collective-permute-start | bytes 983048 | tf_op jit(solution)/shard_map/ppermute | solution.py:13
  526.8 21.5 %collective-permute-start.5 = (f32[10,64,128]{2,1,0:T(8,128)S(1)}, f32[10,64,128]{2,1,0:T(8,128)S(1)}, u32[]{:S(2)}, u32[]{:S(2)}) collective-permute-start(f32[10,64,128]{2,1,0:T(8,128)S(1)} %fusion.20), channel_id=1, source_target_pairs={{0,12},{4,16},{8,20},{12,24},{16,28},{20,32},{24,36},{28,40},{32,4... | collective-permute-start | bytes 983048 | tf_op jit(solution)/shard_map/ppermute | solution.py:13
  529.2 19.2 %copy-start.8 = (f32[10]{0:T(128)S(1)}, f32[10]{0:T(128)}, u32[]{:S(2)}) copy-start(f32[10]{0:T(128)} %param.21) | copy-start | bytes 124
  550.1 6.5 %copy-start = (bf16[256,640]{0,1:T(8,128)(2,1)S(1)}, bf16[256,640]{0,1:T(8,128)(2,1)}, u32[]{:S(2)}) copy-start(bf16[256,640]{0,1:T(8,128)(2,1)} %get-tuple-element.20) | copy-start | bytes 983044
  552.5 12.9 %all-to-all-start.2 = ((bf16[2,4,64,640]{3,2,0,1:T(8,128)(2,1)}), bf16[2,4,64,640]{3,2,0,1:T(8,128)(2,1)S(1)}, u32[]{:S(2)}, u32[]{:S(2)}) async-start(bf16[2,4,64,640]{3,2,0,1:T(8,128)(2,1)} %copy.76), calls=%async_computation.2 | async-start | bytes 1310720 | tf_op jit(solution)/shard_map/all_to_all | solution.py:185
  566.5 0.7 copy-start.3
